TPU v7x, 512 devices: a whole 4x8x8 slice. The times are simulated.
512 devices in a mesh: kv: 16 (over z, core), ep: 32 (over x, y).
Axes of the slice: x: 4, y: 8, z: 8, core: 2. Of those that a mesh axis runs over, the one named last changes fastest.
Arguments:
- queries: bfloat16 [32, 64, 2048], P('ep'), may hold values from -12 to 12
- new_keys: bfloat16 [32, 64, 512], P('ep'), may hold values from -12 to 12
- new_values: bfloat16 [32, 64, 512], P('ep'), may hold values from -6 to 6
- cache_keys: bfloat16 [32, 64, 128, 512], P('ep', 'kv'), may hold values from -12 to 12
- cache_values: bfloat16 [32, 64, 128, 512], P('ep', 'kv'), may hold values from -10 to 10
- page_table: int32 [32, 64], P('ep'), may hold values from 0 to 63, each once within a row
- cached_len: int32 [32], P('ep'), may hold values from 1 to 8192, 65536 in all
- moe_rows: bfloat16 [1024, 4096], P('ep'), may hold values from -6 to 6
- expert_ids: int32 [1024, 2], P('ep'), may hold values from 0 to 7, all different within a row; in each aligned block of 32 rows (0 to 31, 32 to 63, ...) at most 16 rows name the same one
- gate_probs: float32 [1024, 2], P('ep'), may hold values from 0.1 to 0.9
- w_gate: bfloat16 [32, 4096, 2048], P('ep', None, 'kv'), may hold values from -0.09375 to 0.09375
- w_up: bfloat16 [32, 4096, 2048], P('ep', None, 'kv'), may hold values from -0.09375 to 0.09375
- w_down: bfloat16 [32, 2048, 4096], P('ep', 'kv'), may hold values from -0.09375 to 0.09375
Outputs:
- attn_out: bfloat16 [32, 64, 2048], P('ep')
- moe_out: bfloat16 [1024, 4096], P('ep', 'kv')
Inputs may be any that keep to these rules, and one draw needn't show every extreme that they name: `page_table`: each row is a permutation of the 64 slots of its request. `cached_len`: cached positions at or past a request's length hold no data. `expert_ids`: each row names 2 different experts; among the 32 rows of one ep index no expert is named more than 16 times, and this bound is reached.
All inputs are finite; a program needn't handle non-finite values. No bound on the sum of `cached_len` on one device may be relied on, other than what follows from the above.
Results may differ from a plain program's by a relative error of at most 0.0085.
Values may be sent and summed in bfloat16 or wider, within the bound.
No kernel may reach another device: no remote copies, remote signals or barrier semaphores. Data moves between devices by JAX's collectives and lax.ppermute only.
A program may use at most 128 MiB of HBM per device.

v0:
```python
import math
import jax
import jax.numpy as jnp
from jax import lax
from jax.sharding import PartitionSpec as P

HD = 128
EXPERTS = 8
TOP = 2
HQ = 16
KVH = 4
PAGE = 128
POOL_DEV = 4
CAP = 16
ROPE_BASE = 10000.0
MASKED = -1e30


def rotary(values, positions):
    half_width = values.shape[-1] // 2
    indices = jnp.arange(half_width, dtype=jnp.float32)
    frequency = jnp.power(ROPE_BASE, -2.0 * indices / values.shape[-1])
    angles = positions.astype(jnp.float32)[:, None] * frequency[None, :]
    cosine = jnp.cos(angles)[:, None, :]
    sine_part = jnp.sin(angles)[:, None, :]
    lower_half = values[..., :half_width]
    upper_half = values[..., half_width:]
    return jnp.concatenate(
        [
            lower_half * cosine - upper_half * sine_part,
            upper_half * cosine + lower_half * sine_part,
        ],
        axis=-1,
    )


def on_device(
    queries,
    new_keys,
    new_values,
    cache_keys,
    cache_values,
    page_table,
    cached_len,
    moe_rows,
    expert_ids,
    gate_probs,
    w_gate,
    w_up,
    w_down,
):
    kv_index = lax.axis_index("kv")
    kv_count = lax.axis_size("kv")
    all_rows = queries.shape[1]
    block_rows = all_rows // kv_count
    length = cached_len[0]
    group_size = HQ // KVH
    score_scale = 1.0 / math.sqrt(HD)
    slot_ids = kv_index * POOL_DEV + jnp.arange(POOL_DEV, dtype=jnp.int32)
    matches = (page_table[0][:, None] == slot_ids[None, :]).astype(jnp.int32)
    page_index = jnp.sum(
        matches * jnp.arange(page_table.shape[1], dtype=jnp.int32)[:, None], axis=0
    )
    cached_pos = (page_index[:, None] * PAGE + jnp.arange(PAGE, dtype=jnp.int32)[None, :]).reshape(
        -1
    )
    block_start = kv_index * block_rows
    own_pos = length + block_start + jnp.arange(block_rows, dtype=jnp.int32)
    key_block = lax.dynamic_slice_in_dim(new_keys[0], block_start, block_rows, 0)
    value_block = lax.dynamic_slice_in_dim(new_values[0], block_start, block_rows, 0)
    own_keys = rotary(key_block.astype(jnp.float32).reshape(block_rows, KVH, HD), own_pos).astype(
        jnp.bfloat16
    )
    local_keys = jnp.concatenate([cache_keys[0].reshape(-1, KVH, HD), own_keys], axis=0)
    local_values = jnp.concatenate(
        [cache_values[0].reshape(-1, KVH, HD), value_block.reshape(block_rows, KVH, HD)], axis=0
    )
    key_pos = jnp.concatenate([cached_pos, own_pos])
    live_keys = jnp.concatenate([cached_pos < length, jnp.ones((block_rows,), jnp.bool_)])
    positions = length + jnp.arange(all_rows, dtype=jnp.int32)
    rotated = rotary(queries[0].astype(jnp.float32).reshape(all_rows, HQ, HD), positions).astype(
        jnp.bfloat16
    )
    grouped = rotated.reshape(all_rows, KVH, group_size, HD)
    scores = (
        jnp.einsum("nkgd,mkd->nkgm", grouped, local_keys, preferred_element_type=jnp.float32)
        * score_scale
    )
    usable = (live_keys[None, :] & (key_pos[None, :] <= positions[:, None]))[:, None, None, :]
    scores = jnp.where(usable, scores, MASKED)
    part_high = jnp.max(scores, axis=-1)
    highest = lax.pmax(part_high, "kv")
    weights = jnp.where(usable, jnp.exp(scores - highest[..., None]), 0.0)
    part_total = jnp.sum(weights, axis=-1)
    part_blend = jnp.einsum(
        "nkgm,mkd->nkgd",
        weights.astype(jnp.bfloat16),
        local_values,
        preferred_element_type=jnp.float32,
    )
    total_row = jnp.pad(part_total.reshape(1, -1), ((0, 0), (0, HQ * HD - all_rows * HQ)))
    packed = lax.psum(
        jnp.concatenate([part_blend.reshape(all_rows, HQ * HD), total_row], axis=0), "kv"
    )
    row_total = packed[all_rows, : all_rows * HQ].reshape(all_rows, HQ)
    blended = packed[:all_rows].reshape(all_rows, HQ, HD)
    attn_out = (blended / row_total[..., None]).reshape(1, all_rows, HQ * HD).astype(jnp.bfloat16)
    ep_count = lax.axis_size("ep")
    share_count = ep_count // EXPERTS
    tok_rows = moe_rows.shape[0]
    slot_total = ep_count * CAP
    flat_ids = expert_ids.reshape(-1)
    one_hot = (flat_ids[:, None] == jnp.arange(EXPERTS, dtype=jnp.int32)[None, :]).astype(jnp.int32)
    earlier = jnp.cumsum(one_hot, axis=0) - one_hot
    slot_rank = jnp.sum(earlier * one_hot, axis=1)
    slot_index = jnp.arange(slot_total, dtype=jnp.int32)
    dest_expert = slot_index // CAP // share_count
    dest_slot = slot_index % CAP
    matched = (flat_ids[None, :] == dest_expert[:, None]) & (
        slot_rank[None, :] == dest_slot[:, None]
    )
    select = jnp.sum(matched.astype(jnp.float32).reshape(slot_total, tok_rows, TOP), axis=2).astype(
        jnp.bfloat16
    )
    weight_map = jnp.sum(
        jnp.where(matched, gate_probs.reshape(-1)[None, :], 0.0).reshape(slot_total, tok_rows, TOP),
        axis=2,
    )
    col_width = moe_rows.shape[1] // kv_count
    rows_cols = lax.dynamic_slice_in_dim(moe_rows, kv_index * col_width, col_width, 1)
    outgoing = (
        jnp.dot(select, rows_cols, preferred_element_type=jnp.float32)
        .astype(jnp.bfloat16)
        .reshape(ep_count, CAP, -1)
    )
    arrived_cols = lax.all_to_all(outgoing, "ep", split_axis=0, concat_axis=0, tiled=True).reshape(
        slot_total, -1
    )
    arrived = lax.all_gather(arrived_cols, "kv", axis=1, tiled=True)
    gate_proj = jnp.dot(arrived, w_gate[0], preferred_element_type=jnp.float32)
    up_proj = jnp.dot(arrived, w_up[0], preferred_element_type=jnp.float32)
    hidden = (jax.nn.silu(gate_proj) * up_proj).astype(jnp.bfloat16)
    out_width = w_down.shape[2] // kv_count
    down_split = w_down[0].reshape(w_down.shape[1], kv_count, out_width)
    down_cols = lax.all_to_all(down_split, "kv", split_axis=1, concat_axis=0, tiled=True).reshape(
        -1, out_width
    )
    summed = jnp.dot(
        lax.all_gather(hidden, "kv", axis=1, tiled=True),
        down_cols,
        preferred_element_type=jnp.float32,
    )
    returned = (
        lax.all_to_all(
            summed.reshape(ep_count, CAP, -1).astype(jnp.bfloat16),
            "ep",
            split_axis=0,
            concat_axis=0,
            tiled=True,
        )
        .astype(jnp.float32)
        .reshape(slot_total, -1)
    )
    moe_out = jnp.dot(
        weight_map.T, returned, precision=lax.Precision.HIGHEST, preferred_element_type=jnp.float32
    ).astype(jnp.bfloat16)
    return (attn_out, moe_out)


def solution(mesh):
    return jax.shard_map(
        on_device,
        mesh=mesh,
        in_specs=(
            P("ep", None, None),
            P("ep", None, None),
            P("ep", None, None),
            P("ep", "kv", None, None),
            P("ep", "kv", None, None),
            P("ep", None),
            P("ep"),
            P("ep", None),
            P("ep", None),
            P("ep", None),
            P("ep", None, "kv"),
            P("ep", None, "kv"),
            P("ep", "kv", None),
        ),
        out_specs=(P("ep", None, None), P("ep", "kv")),
        check_vma=False,
    )
```

profile of v0, /device:TPU:2, one launch (start us, length us, event | category | flops | bytes accessed | tf_op | source)
XLA Modules:
  0.0 277.6 jit_solution(767339811898479776)
XLA Ops:
  7.2 0.8 copy.46
  8.1 0.1 eq.71
  8.2 0.1 fusion.26
  8.3 0.1 reduce_window_sum.11
  8.4 0.2 select_reduce_fusion.1
  8.5 0.1 eq.75
  8.7 0.1 copy.47
  8.7 0.8 convert_reduce_fusion
  9.6 1.0 convolution_convert_fusion
  10.5 21.4 %all_to_all.25 = bf16[32,16,256]{2,1,0:T(8,128)(2,1)} all-to-all(bf16[32,16,256]{2,1,0:T(8,128)(2,1)S(1)} %bitcast.94), channel_id=1, replica_groups=mesh['kv'=16,'ep'=32] {'ep'}, dimensions={0} | all-to-all | bytes 524288 | tf_op jit(solution)/shard_map/all_to_all | solution.py:136
  32.0 1.5 copy.55
  33.5 1.3 copy.48
  34.8 10.5 %all-to-all-start.1 = ((bf16[128,16,256]{2,0,1:T(8,128)(2,1)}), bf16[128,16,256]{2,0,1:T(8,128)(2,1)S(1)}, u32[]{:S(2)}, u32[]{:S(2)}) async-start(bf16[128,16,256]{2,0,1:T(8,128)(2,1)} %copy.48), calls=%async_computation.1 | async-start | bytes 2097152 | tf_op jit(solution)/shard_map/all_to_all | solution.py:145
  46.1 0.1 copy.53
  46.2 1.2 reshape_squeeze.10
  47.4 0.9 copy.41
  48.3 0.2 select_reduce_fusion.2
  48.5 55.1 %all-gather.3.cloned.1.call-done = bf16[512,4096]{1,0:T(8,128)(2,1)} async-done(((bf16[512,256]{1,0:T(8,128)(2,1)}), bf16[512,4096]{1,0:T(8,128)(2,1)}) %all-gather.3.cloned.1.call-update) | async-done | bytes 4194320 | tf_op jit(solution)/shard_map/all_gather | solution.py:139
  103.5 3.6 %fusion.11 = f32[512,128]{1,0:T(8,128)S(1)} fusion(bf16[512,4096]{1,0:T(8,128)(2,1)} %all-gather.3.cloned.1.call-done, bf16[1,4096,128]{2,1,0:T(8,128)(2,1)S(1)} %copy-done), kind=kOutput, calls=%fused_computation.14 | convolution fusion | flops 536870912 | bytes 5505024 | tf_op jit(solution)/shard_map/dot_general | solution.py:140
  107.1 0.1 copy-done.5
  107.3 1.9 fusion.9
  109.3 0.1 broadcast_compare_fusion
  109.5 0.7 bitcast_convert_fusion
  110.2 0.1 multiply_cosine_fusion.1
  110.3 0.1 compare_and_fusion
  110.4 0.2 multiply_cosine_fusion
  110.6 0.1 subtract_convert_fusion.1
  110.7 0.2 fusion.48
  110.9 0.3 subtract_convert_fusion
  111.2 2.2 fusion
  113.5 24.3 %pmax.7 = f32[64,4,4]{0,2,1:T(4,128)S(1)} all-reduce(f32[64,4,4]{0,2,1:T(4,128)S(1)} %get-tuple-element.14), channel_id=1, replica_groups=mesh['kv'=16,'ep'=32] {'kv'}, use_global_device_ids=true, to_apply=%region_2.3 | all-reduce | flops 1024 | bytes 8192 | tf_op jit(solution)/shard_map/pmax | solution.py:92
  137.8 2.6 fusion.1
  140.4 0.1 copy.45
  140.5 0.2 reshape.299
  140.7 0.1 reshape_squeeze.9
  140.9 0.7 dynamic-slice_bitcast_fusion
  141.6 2.5 fusion.6
  144.1 0.3 copy.44
  144.5 0.2 reshape.298
  144.7 0.9 select_maximum_fusion
  145.6 3.0 %all-gather.5.cloned.1.call-done = bf16[512,2048]{1,0:T(8,128)(2,1)} async-done(((bf16[512,128]{1,0:T(8,128)(2,1)}), bf16[512,2048]{1,0:T(8,128)(2,1)}) %all-gather.5.cloned.1.call-update) | async-done | bytes 2097168 | tf_op jit(solution)/shard_map/all_gather | solution.py:149
  148.6 3.0 %convolution_convert_fusion.1 = bf16[32,16,256]{2,1,0:T(8,128)(2,1)} fusion(bf16[32,16,2048]{2,1,0:T(8,128)(2,1)} %bitcast.97, bf16[2048,256,1]{1,0,2:T(8,128)(2,1)S(1)} %bitcast.91), kind=kOutput, calls=%fused_computation.9 | convolution fusion | flops 537001984 | bytes 3407872 | tf_op jit(solution)/shard_map/dot_general | solution.py:148
  151.6 9.9 %all-to-all-start.2 = ((bf16[32,16,256]{2,1,0:T(8,128)(2,1)}), bf16[32,16,256]{2,1,0:T(8,128)(2,1)S(1)}, u32[]{:S(2)}, u32[]{:S(2)}) async-start(bf16[32,16,256]{2,1,0:T(8,128)(2,1)} %convolution_convert_fusion.1), calls=%async_computation.2 | async-start | bytes 524288 | tf_op jit(solution)/shard_map/all_to_all | solution.py:154
  161.5 105.7 %all-reduce.4.cloned.1.call-done = f32[65,2048]{1,0:T(8,128)} async-done(((f32[65,2048]{1,0:T(8,128)}), f32[65,2048]{1,0:T(8,128)}) %all-reduce.4.cloned.1.call-update) | async-done | bytes 532496 | tf_op jit(solution)/shard_map/psum | solution.py:102
  267.2 0.8 slice_reduce_fusion
  268.0 0.2 div.46
  268.2 1.9 fusion.24
  270.2 0.9 convolution_convert_fusion.2
  (33 shorter events, 0.5 us)
Async XLA Ops:
  7.2 96.4 %copy-start = (bf16[1,4096,128]{2,1,0:T(8,128)(2,1)S(1)}, bf16[1,4096,128]{2,1,0:T(8,128)(2,1)}, u32[]{:S(2)}) copy-start(bf16[1,4096,128]{2,1,0:T(8,128)(2,1)} %param.23) | copy-start | bytes 3145732
  7.2 96.3 %all-gather.3.cloned.1.call-start = ((), (), s32[]{:S(2)}) async-start(), calls=%async_computation.4 | async-start | bytes 4456448 | tf_op jit(solution)/shard_map/all_gather | solution.py:139
  33.5 12.6 %copy-start.4 = (bf16[1,64,2048]{2,1,0:T(8,128)(2,1)S(1)}, bf16[1,64,2048]{2,1,0:T(8,128)(2,1)}, u32[]{:S(2)}) copy-start(bf16[1,64,2048]{2,1,0:T(8,128)(2,1)} %param.13) | copy-start | bytes 786436
  34.8 13.5 %copy-start.6 = (s32[1,64]{1,0:T(1,128)S(1)}, s32[1,64]{1,0:T(1,128)}, u32[]{:S(2)}) copy-start(s32[1,64]{1,0:T(1,128)} %param.18) | copy-start | bytes 772
  34.8 110.8 %all-to-all-start.1 = ((bf16[128,16,256]{2,0,1:T(8,128)(2,1)}), bf16[128,16,256]{2,0,1:T(8,128)(2,1)S(1)}, u32[]{:S(2)}, u32[]{:S(2)}) async-start(bf16[128,16,256]{2,0,1:T(8,128)(2,1)} %copy.48), calls=%async_computation.1 | async-start | bytes 2097152 | tf_op jit(solution)/shard_map/all_to_all | solution.py:145
  45.4 103.2 %all-gather.5.cloned.1.call-start = ((), (), s32[]{:S(2)}) async-start(), calls=%async_computation.5 | async-start | bytes 2228224 | tf_op jit(solution)/shard_map/all_gather | solution.py:149
  103.5 3.6 %copy-start.1 = (bf16[512,4096]{1,0:T(8,128)(2,1)S(1)}, bf16[512,4096]{1,0:T(8,128)(2,1)}, u32[]{:S(2)}) copy-start(bf16[512,4096]{1,0:T(8,128)(2,1)} %all-gather.3.cloned.1.call-done) | copy-start | bytes 12582916
  103.5 3.7 %copy-start.5 = (bf16[1,4096,128]{2,1,0:T(8,128)(2,1)S(1)}, bf16[1,4096,128]{2,1,0:T(8,128)(2,1)}, u32[]{:S(2)}) copy-start(bf16[1,4096,128]{2,1,0:T(8,128)(2,1)} %param.24) | copy-start | bytes 3145732
  109.2 2.0 copy-start.3
  109.2 158.0 %all-reduce.4.cloned.1.call-start = ((), (), s32[]{:S(2)}) async-start(), calls=%async_computation.3 | async-start | bytes 1179648 | tf_op jit(solution)/shard_map/psum | solution.py:102
  111.2 29.5 %copy-start.2 = (bf16[1,4,128,512]{3,2,1,0:T(8,128)(2,1)S(1)}, bf16[1,4,128,512]{3,2,1,0:T(8,128)(2,1)}, u32[]{:S(2)}) copy-start(bf16[1,4,128,512]{3,2,1,0:T(8,128)(2,1)} %param.17) | copy-start | bytes 1572868
  151.6 118.6 %all-to-all-start.2 = ((bf16[32,16,256]{2,1,0:T(8,128)(2,1)}), bf16[32,16,256]{2,1,0:T(8,128)(2,1)S(1)}, u32[]{:S(2)}, u32[]{:S(2)}) async-start(bf16[32,16,256]{2,1,0:T(8,128)(2,1)} %convolution_convert_fusion.1), calls=%async_computation.2 | async-start | bytes 524288 | tf_op jit(solution)/shard_map/all_to_all | solution.py:154
Sparse Core Ops, SparseCore 0:
  32.1 71.3 all-gather.2
  109.3 39.2 all-gather.4
  150.9 116.2 all-reduce.3
where the time goes:
time: 278 us
  waiting for transfers between devices  164 us (59%)
  blocking collectives  45.7 us (16%)
  starting transfers between devices  20.6 us (7%)
  matrix products  15 us (5%)
  between operations  14.7 us (5%)
  local copies, waits for them, and re-layouts  9.25 us (3%)
  other arithmetic  8.53 us (3%)
    psum x1, waiting for transfers between devices, on_device(): lax.psum(jnp.concatenate([part_blend.reshape(all_rows, HQ * HD), total_ro...  106 us
    all_gather x1, waiting for transfers between devices, on_device(): arrived = lax.all_gather(arrived_cols, 'kv', axis=1, tiled=True)  55.1 us
    pmax x1, blocking collectives, on_device(): highest = lax.pmax(part_high, 'kv')  24.3 us
    all_to_all x1, blocking collectives, on_device(): lax.all_to_all(outgoing, 'ep', split_axis=0, concat_axis=0, tiled=True)  21.4 us
    all_to_all x1, starting transfers between devices, on_device(): lax.all_to_all(down_split, 'kv', split_axis=1, concat_axis=0, tiled=True)  10.5 us
    all_to_all x1, starting transfers between devices, on_device(): lax.all_to_all(summed.reshape(ep_count, CAP, -1).astype(jnp.bfloat16), 'e...  9.89 us
  transfers between devices with their start and end apart: 5, of which 3 were waited for; matrix products, arithmetic and copies ran while one was open for 10% of the time, Pallas kernels for 0%

commit v1 on v0

--- a/solution.py
+++ b/solution.py
@@ -14,6 +14,11 @@
 CAP = 16
 ROPE_BASE = 10000.0
 MASKED = -1e30
+
+
+def _press_ways(sample):
+    t_next = lax.all_gather(sample, "kv").sum(axis=0)
+    return t_next
 
 
 def rotary(values, positions):
@@ -99,8 +104,8 @@
         preferred_element_type=jnp.float32,
     )
     total_row = jnp.pad(part_total.reshape(1, -1), ((0, 0), (0, HQ * HD - all_rows * HQ)))
-    packed = lax.psum(
-        jnp.concatenate([part_blend.reshape(all_rows, HQ * HD), total_row], axis=0), "kv"
+    packed = _press_ways(
+        jnp.concatenate([part_blend.reshape(all_rows, HQ * HD), total_row], axis=0)
     )
     row_total = packed[all_rows, : all_rows * HQ].reshape(all_rows, HQ)
     blended = packed[:all_rows].reshape(all_rows, HQ, HD)

time: 278 us -> 220 us (0.79)
  the two profiles are of different devices: /device:TPU:2 before, /device:TPU:1 now
where the time goes in v1:
time: 220 us; the launch traced here: 219 us
  blocking collectives  103 us (47%)
  waiting for transfers between devices  68.5 us (31%)
  between operations  14.7 us (7%)
  matrix products  14.3 us (6%)
  other arithmetic  13 us (6%)
  local copies, waits for them, and re-layouts  5.28 us (2%)
    all_gather x1, waiting for transfers between devices, on_device(): arrived = lax.all_gather(arrived_cols, 'kv', axis=1, tiled=True)  52.2 us
    all_to_all x1, blocking collectives, on_device(): lax.all_to_all(down_split, 'kv', split_axis=1, concat_axis=0, tiled=True)  38.9 us
    pmax x1, blocking collectives, on_device(): highest = lax.pmax(part_high, 'kv')  23.6 us
    all_to_all x1, blocking collectives, on_device(): lax.all_to_all(summed.reshape(ep_count, CAP, -1).astype(jnp.bfloat16), 'e...  20.5 us
    all_to_all x1, blocking collectives, on_device(): lax.all_to_all(outgoing, 'ep', split_axis=0, concat_axis=0, tiled=True)  20.1 us
    all_gather x1, waiting for transfers between devices, _press_ways(): t_next = lax.all_gather(sample, 'kv').sum(axis=0)  16.3 us
    reduce_sum x1, other arithmetic, _press_ways(): t_next = lax.all_gather(sample, 'kv').sum(axis=0)  4.44 us
  transfers between devices with their start and end apart: 3, of which 2 were waited for; matrix products, arithmetic and copies ran while one was open for 8% of the time, Pallas kernels for 0%

profile of v1, /device:TPU:1, one launch (start us, length us, event | category | flops | bytes accessed | tf_op | source)
XLA Modules:
  0.0 219.0 jit_solution(12370066087555320939)
XLA Ops:
  7.3 0.9 copy.46
  8.1 0.1 eq.71
  8.3 0.1 fusion.27
  8.3 0.1 reduce_window_sum.11
  8.4 0.2 select_reduce_fusion.1
  8.6 0.1 eq.75
  8.7 0.1 copy.47
  8.8 0.8 convert_reduce_fusion
  9.6 1.0 convolution_convert_fusion
  10.6 20.1 %all_to_all.25 = bf16[32,16,256]{2,1,0:T(8,128)(2,1)} all-to-all(bf16[32,16,256]{2,1,0:T(8,128)(2,1)S(1)} %bitcast.96), channel_id=1, replica_groups=mesh['kv'=16,'ep'=32] {'ep'}, dimensions={0} | all-to-all | bytes 524288 | tf_op jit(solution)/shard_map/all_to_all | solution.py:141
  31.4 1.0 convert_bitcast_fusion
  32.4 0.1 copy.53
  32.5 0.1 reshape_squeeze.10
  32.6 0.9 copy.41
  33.5 0.1 reshape_squeeze.9
  33.7 0.2 select_reduce_fusion.2
  33.9 52.2 %all-gather.6.cloned.1.call-done = bf16[512,4096]{1,0:T(8,128)(2,1)} async-done(((bf16[512,256]{1,0:T(8,128)(2,1)}), bf16[512,4096]{1,0:T(8,128)(2,1)}) %all-gather.6.cloned.1.call-update) | async-done | bytes 4194320 | tf_op jit(solution)/shard_map/all_gather | solution.py:144
  86.1 3.6 %fusion.11 = f32[512,128]{1,0:T(8,128)S(1)} fusion(bf16[512,4096]{1,0:T(8,128)(2,1)} %all-gather.6.cloned.1.call-done, bf16[1,4096,128]{2,1,0:T(8,128)(2,1)S(1)} %copy-done), kind=kOutput, calls=%fused_computation.14 | convolution fusion | flops 536870912 | bytes 5505024 | tf_op jit(solution)/shard_map/dot_general | solution.py:145
  89.7 0.1 copy-done.6
  89.9 1.9 fusion.9
  91.8 0.1 broadcast_compare_fusion
  92.0 0.7 bitcast_convert_fusion
  92.7 0.1 multiply_cosine_fusion.1
  92.9 0.1 subtract_convert_fusion.1
  92.9 0.1 compare_and_fusion
  93.0 0.2 multiply_cosine_fusion
  93.2 0.2 fusion.49
  93.4 0.3 subtract_convert_fusion
  93.8 2.2 fusion
  96.0 23.6 %pmax.7 = f32[64,4,4]{0,2,1:T(4,128)S(1)} all-reduce(f32[64,4,4]{0,2,1:T(4,128)S(1)} %get-tuple-element.14), channel_id=1, replica_groups=mesh['kv'=16,'ep'=32] {'kv'}, use_global_device_ids=true, to_apply=%region_2.3 | all-reduce | flops 1024 | bytes 8192 | tf_op jit(solution)/shard_map/pmax | solution.py:97
  119.6 0.7 dynamic-slice_bitcast_fusion
  120.3 2.5 %fusion.6 = f32[64,4,4,128]{3,0,2,1:T(8,128)S(1)} fusion(f32[4,516,64,4]{1,2,3,0:T(8,128)} %get-tuple-element.15, f32[64,4,4]{0,2,1:T(4,128)S(1)} %pmax.7, pred[64,516]{1,0:T(8,128)(4,1)S(1)} %compare_and_fusion, bf16[4,4,128]{2,0,1:T(4,128)(2,1)S(1)} %dynamic-slice_bitcast_fusion, bf16[512,4,128]{2,0,1:T(8,128)(2,1)S(1)} %copy.40), kind=kOutput, calls=%fused_computation.7 | convolution fusion | flops 138964992 | bytes 3203328 | tf_op jit(solution)/shard_map/nkgm,mkd->nkgd/dot_general | solution.py:100
  122.8 0.3 copy.44
  123.2 0.2 reshape.298
  123.4 2.7 %fusion.1 = f32[64,4,4]{0,2,1:T(4,128)S(1)} fusion(f32[4,516,64,4]{1,2,3,0:T(8,128)} %get-tuple-element.15, f32[64,4,4]{0,2,1:T(4,128)S(1)} %pmax.7, pred[64,516]{1,0:T(8,128)(4,1)S(1)} %compare_and_fusion), kind=kLoop, calls=%fused_computation.3 | loop fusion | flops 2640896 | bytes 2154752 | tf_op jit(solution)/shard_map/reduce_sum | solution.py:99
  126.2 0.1 copy.45
  126.3 0.2 reshape.299
  126.5 0.9 fusion.13
  127.4 0.2 copy.55
  127.6 0.3 copy.48
  128.0 38.9 %all_to_all.26 = bf16[128,16,256]{2,0,1:T(8,128)(2,1)S(1)} all-to-all(bf16[128,16,256]{2,0,1:T(8,128)(2,1)S(1)} %copy.48), channel_id=1, replica_groups=mesh['kv'=16,'ep'=32] {'kv'}, dimensions={1} | all-to-all | bytes 2097152 | tf_op jit(solution)/shard_map/all_to_all | solution.py:150
  166.8 2.4 %convolution_convert_fusion.1 = bf16[32,16,256]{2,1,0:T(8,128)(2,1)S(1)} fusion(bf16[32,16,2048]{2,1,0:T(8,128)(2,1)} %bitcast.99, bf16[2048,256,1]{1,0,2:T(8,128)(2,1)S(1)} %bitcast.93), kind=kOutput, calls=%fused_computation.9 | convolution fusion | flops 537001984 | bytes 3407872 | tf_op jit(solution)/shard_map/dot_general | solution.py:153
  169.2 20.5 %all_to_all.27 = bf16[32,16,256]{2,1,0:T(8,128)(2,1)S(1)} all-to-all(bf16[32,16,256]{2,1,0:T(8,128)(2,1)S(1)} %convolution_convert_fusion.1), channel_id=1, replica_groups=mesh['kv'=16,'ep'=32] {'ep'}, dimensions={0} | all-to-all | bytes 524288 | tf_op jit(solution)/shard_map/all_to_all | solution.py:159
  189.7 0.9 convolution_convert_fusion.2
  190.6 16.3 %all-gather.10.cloned.1.call-done = f32[16,65,2048]{2,1,0:T(8,128)} async-done(((f32[1,65,2048]{2,1,0:T(8,128)}), f32[16,65,2048]{2,1,0:T(8,128)}) %all-gather.10.cloned.1.call-update) | async-done | bytes 8519696 | tf_op jit(solution)/shard_map/all_gather | solution.py:20
  206.8 4.4 %reduce_sum.56 = f32[65,2048]{1,0:T(8,128)S(1)} reduce(f32[16,65,2048]{2,1,0:T(8,128)} %all-gather.10.cloned.1.call-done, f32[]{:T(128)} %constant.75.clone.1), dimensions={0}, to_apply=%region_4.5 | reduce | flops 1996800 | bytes 9052164 | tf_op jit(solution)/shard_map/reduce_sum | solution.py:20
  211.4 0.2 div.46
  211.6 0.9 fusion.25
  (34 shorter events, 0.5 us)
Async XLA Ops:
  7.2 78.9 %copy-start = (bf16[1,4096,128]{2,1,0:T(8,128)(2,1)S(1)}, bf16[1,4096,128]{2,1,0:T(8,128)(2,1)}, u32[]{:S(2)}) copy-start(bf16[1,4096,128]{2,1,0:T(8,128)(2,1)} %param.23) | copy-start | bytes 3145732
  7.2 25.3 %copy-start.3 = (bf16[1,4,128,512]{3,2,1,0:T(8,128)(2,1)S(1)}, bf16[1,4,128,512]{3,2,1,0:T(8,128)(2,1)}, u32[]{:S(2)}) copy-start(bf16[1,4,128,512]{3,2,1,0:T(8,128)(2,1)} %param.16) | copy-start | bytes 1572868
  7.2 78.9 %all-gather.6.cloned.1.call-start = ((), (), s32[]{:S(2)}) async-start(), calls=%async_computation.3 | async-start | bytes 4456448 | tf_op jit(solution)/shard_map/all_gather | solution.py:144
  8.4 25.1 %copy-start.4 = (bf16[1,4,128,512]{3,2,1,0:T(8,128)(2,1)S(1)}, bf16[1,4,128,512]{3,2,1,0:T(8,128)(2,1)}, u32[]{:S(2)}) copy-start(bf16[1,4,128,512]{3,2,1,0:T(8,128)(2,1)} %param.17) | copy-start | bytes 1572868
  30.7 136.1 %all-gather.8.cloned.1.call-start = ((), (), s32[]{:S(2)}) async-start(), calls=%async_computation.4 | async-start | bytes 2228224 | tf_op jit(solution)/shard_map/all_gather | solution.py:154
  32.4 1.3 copy-start.7
  86.1 3.6 %copy-start.1 = (bf16[512,4096]{1,0:T(8,128)(2,1)S(1)}, bf16[512,4096]{1,0:T(8,128)(2,1)}, u32[]{:S(2)}) copy-start(bf16[512,4096]{1,0:T(8,128)(2,1)} %all-gather.6.cloned.1.call-done) | copy-start | bytes 12582916
  86.1 3.7 %copy-start.6 = (bf16[1,4096,128]{2,1,0:T(8,128)(2,1)S(1)}, bf16[1,4096,128]{2,1,0:T(8,128)(2,1)}, u32[]{:S(2)}) copy-start(bf16[1,4096,128]{2,1,0:T(8,128)(2,1)} %param.24) | copy-start | bytes 3145732
  91.8 2.0 copy-start.5
  91.8 115.0 %all-gather.10.cloned.1.call-start = ((), (), s32[]{:S(2)}) async-start(), calls=%async_computation.5 | async-start | bytes 10027008 | tf_op jit(solution)/shard_map/all_gather | solution.py:20
  123.2 4.2 %copy-start.2 = (bf16[1,128,4096]{2,1,0:T(8,128)(2,1)S(1)}, bf16[1,128,4096]{2,1,0:T(8,128)(2,1)}, u32[]{:S(2)}) copy-start(bf16[1,128,4096]{2,1,0:T(8,128)(2,1)} %param.25) | copy-start | bytes 3145732
Sparse Core Ops, SparseCore 0:
  30.8 55.2 all-gather.5
  91.9 41.9 all-gather.7
  136.0 70.7 all-gather.9
